TPU v7x, 32 devices: a whole 2x2x4 slice. The times are simulated.
32 devices in a mesh: pair: 4 (over z), gen: 8 (over y, x, core).
Axes of the slice: x: 2, y: 2, z: 4, core: 2. Of those that a mesh axis runs over, the one named last changes fastest.
Arguments:
- tokens: bfloat16 [32768, 2048], P(('pair', 'gen')), may hold values from -6 to 6
- cotangent: bfloat16 [32768, 256], P(('pair', 'gen')), may hold values from -6 to 6
- block_pair: int32 [32, 1], replicated, may hold values from 0 to 15
- src_lang: int32 [16], replicated, may hold values from 0 to 95
- tgt_lang: int32 [16], replicated, may hold values from 0 to 95
- lang_embed: float32 [96, 512], P(None, 'pair'), may hold values from -5 to 5
- generator: bfloat16 [512, 524288], P('pair', 'gen'), may hold values from -0.005859375 to 0.005859375
Outputs:
- grad_tokens: bfloat16 [32768, 2048], P(('pair', 'gen'))
- grad_generator: bfloat16 [512, 524288], P('pair', 'gen')
- grad_embed: float32 [96, 512], P(None, 'pair')
Inputs may be any that keep to these rules, and one draw needn't show every extreme that they name: `block_pair`: every pair owns at least one block; block counts per pair are uneven.
All inputs are finite; a program needn't handle non-finite values.
Results may differ from a plain program's by a relative error of at most 0.007.
Values may be sent and summed in bfloat16 or wider, within the bound.
No kernel may reach another device: no remote copies, remote signals or barrier semaphores. Data moves between devices by JAX's collectives and lax.ppermute only.
A program may use at most 128 MiB of HBM per device.

v0:
```python
import jax
import jax.numpy as jnp
from jax import lax
from jax.sharding import PartitionSpec as P

BLK = 1024


def shards(tokens, cotangent, block_pair, src_lang, tgt_lang, lang_embed, generator):
    gen_count = lax.axis_size("gen")
    pair_index = lax.axis_index("pair")
    blocks_here = tokens.shape[0] // BLK
    model_width = tokens.shape[1]
    adapter_rank = cotangent.shape[1]
    languages = lang_embed.shape[0]
    pair_count = src_lang.shape[0]
    lang_ids = jnp.arange(languages, dtype=jnp.int32)
    hot_both = (src_lang[:, None] == lang_ids[None, :]).astype(jnp.float32) + (
        tgt_lang[:, None] == lang_ids[None, :]
    ).astype(jnp.float32)
    pair_embed = jnp.dot(hot_both, lang_embed, precision=lax.Precision.HIGHEST).astype(jnp.bfloat16)
    partial_value = jnp.dot(pair_embed, generator, preferred_element_type=jnp.float32)
    adapter_cols = lax.psum(partial_value, "pair").astype(jnp.bfloat16)
    flat_pairs = block_pair[:, 0]
    row_pairs = lax.dynamic_slice_in_dim(
        flat_pairs, pair_index * (gen_count * blocks_here), gen_count * blocks_here
    )
    send_order = row_pairs.reshape(gen_count, blocks_here).T
    outgoing = jnp.take(adapter_cols, send_order, axis=0).reshape(
        blocks_here, gen_count * adapter_cols.shape[1]
    )
    own_adapters = lax.all_to_all(outgoing, "gen", split_axis=1, concat_axis=1, tiled=True)
    adapters = own_adapters.reshape(blocks_here, model_width, adapter_rank)
    token_blocks = tokens.reshape(blocks_here, BLK, model_width)
    cot_blocks = cotangent.reshape(blocks_here, BLK, adapter_rank)
    hidden = jnp.einsum("btd,bdr->btr", token_blocks, adapters, preferred_element_type=jnp.float32)
    logistic = jax.nn.sigmoid(hidden)
    grad_hidden = (
        cot_blocks.astype(jnp.float32) * logistic * (1.0 + hidden * (1.0 - logistic))
    ).astype(jnp.bfloat16)
    grad_tokens = (
        jnp.einsum("btr,bdr->btd", grad_hidden, adapters, preferred_element_type=jnp.float32)
        .astype(jnp.bfloat16)
        .reshape(tokens.shape)
    )
    outer_grads = jnp.einsum(
        "btd,btr->bdr", token_blocks, grad_hidden, preferred_element_type=jnp.float32
    ).reshape(blocks_here, model_width * adapter_rank)
    returned = lax.all_to_all(outer_grads, "gen", split_axis=1, concat_axis=0, tiled=True)
    pair_ids = jnp.arange(pair_count, dtype=jnp.int32)
    segment_hot = (pair_ids[:, None] == row_pairs[None, :]).astype(jnp.float32)
    row_grad = jnp.dot(segment_hot, returned, precision=lax.Precision.HIGHEST)
    grad_rounded = lax.psum(row_grad, "pair").astype(jnp.bfloat16)
    grad_generator = jnp.einsum(
        "pe,pc->ec", pair_embed, grad_rounded, preferred_element_type=jnp.float32
    ).astype(jnp.bfloat16)
    partial_pair = jnp.einsum(
        "pc,ec->pe", grad_rounded, generator, preferred_element_type=jnp.float32
    )
    grad_pair = lax.psum(partial_pair, "gen")
    grad_embed = jnp.dot(hot_both.T, grad_pair, precision=lax.Precision.HIGHEST)
    return (grad_tokens, grad_generator, grad_embed)


def solution(mesh):
    placed = (
        P(("pair", "gen"), None),
        P(("pair", "gen"), None),
        P(),
        P(),
        P(),
        P(None, "pair"),
        P("pair", "gen"),
    )
    return jax.shard_map(
        shards,
        mesh=mesh,
        in_specs=placed,
        out_specs=(P(("pair", "gen"), None), P("pair", "gen"), P(None, "pair")),
        check_vma=False,
    )
```

profile of v0, /device:TPU:0, one launch (start us, length us, event | category | flops | bytes accessed | tf_op | source)
XLA Modules:
  0.0 421.6 jit_solution(15591775119214140472)
XLA Ops:
  0.6 0.0 copy-start
  0.7 0.7 fusion.16
  1.4 0.7 compare_and_fusion
  2.1 0.0 copy-done
  2.1 0.9 convolution_convert_fusion.2
  3.0 10.1 %fusion.21 = f32[16,65536]{1,0:T(8,128)} fusion(bf16[16,128]{1,0:T(8,128)(2,1)S(1)} %convolution_convert_fusion.2, bf16[128,65536]{1,0:T(8,128)(2,1)} %param.13), kind=kOutput, calls=%fused_computation.39 | convolution fusion | flops 268435456 | bytes 20975616 | tf_op jit(solution)/shard_map/dot_general | solution.py:22
  13.1 149.0 %all-reduce.2 = bf16[16,65536]{1,0:T(8,128)(2,1)S(1)} all-reduce(f32[16,65536]{1,0:T(8,128)} %fusion.21), channel_id=1, replica_groups=mesh['pair'=4,'gen'=8] {'pair'}, use_global_device_ids=true, to_apply=%region_0.0 | all-reduce | flops 1048576 | bytes 6291456 | tf_op jit(solution)/shard_map/psum | solution.py:23
  162.1 1.2 gather_fusion
  163.4 0.2 bitcast_select_fusion
  163.5 1.6 copy.27
  165.2 0.5 broadcast.100
  165.7 7.0 %reduce.2 = bf16[8,65536]{1,0:T(8,128)(2,1)S(1)} reduce(bf16[8,1,65536]{2,1,0:T(2,128)(2,1)S(1)} %bitcast.33, bf16[]{:T(256)} %broadcast.100), dimensions={1}, to_apply=%bitcast.32.reduce_sub_computation | reduce | bytes 2097154
  172.7 0.0 copy-start.4
  172.7 1.9 reshape.166
  174.6 3.8 all-to-all-start
  178.4 0.0 copy-done.4
  178.4 1.0 copy.17
  179.4 14.3 %all-to-all-done = bf16[8,2,32768]{2,1,0:T(2,128)(2,1)S(1)} async-done(((bf16[8,2,32768]{2,1,0:T(2,128)(2,1)}), bf16[8,2,32768]{2,1,0:T(2,128)(2,1)S(1)}, u32[]{:S(2)}, u32[]{:S(2)}) %all-to-all-start) | async-done | bytes 1048608 | tf_op jit(solution)/shard_map/all_to_all | solution.py:32
  193.7 1.0 reshape.167
  194.8 6.0 %bitcast_reduce_fusion = bf16[8,65536]{1,0:T(8,128)(2,1)S(1)} fusion(bf16[8,1,65536]{2,1,0:T(2,128)(2,1)S(1)} %reshape.167), kind=kLoop, calls=%fused_computation.37 | loop fusion | bytes 2097152 | tf_op jit(solution)/shard_map/all_to_all | solution.py:32
  200.8 0.5 reshape.156
  201.3 0.0 copy-start.2
  201.3 0.0 copy-start.5
  201.3 0.0 copy-start.6
  201.3 3.9 convolution_bitcast_fusion.1
  205.2 0.0 copy-done.2
  205.2 0.0 copy-start.9
  205.2 1.0 copy-done.9
  206.2 0.0 copy-done.5
  206.2 0.0 copy-done.6
  206.2 2.9 convolution_bitcast_fusion
  209.1 1.9 copy.19
  211.0 0.0 copy-start.3
  211.0 4.2 all_to_all.20
  215.2 3.9 all-to-all-start.1
  219.0 0.0 copy-done.3
  219.0 5.0 %convolution_convert_fusion.1 = bf16[1024,2048]{1,0:T(8,128)(2,1)} fusion(bf16[2048,256]{1,0:T(8,128)(2,1)S(1)} %copy-done.3, f32[1024,256]{0,1:T(8,128)} %copy-done.9, bf16[1024,256]{0,1:T(8,128)(2,1)} %copy.17), kind=kOutput, calls=%fused_computation.2 | convolution fusion | flops 1078460416 | bytes 6815744 | tf_op jit(solution)/shard_map/btr,bdr->btd/dot_general | solution.py:42
  224.0 21.3 %all-to-all-done.1 = f32[1,8,65536]{2,0,1:T(1,128)S(1)} async-done(((f32[1,8,65536]{2,0,1:T(1,128)}), f32[1,8,65536]{2,0,1:T(1,128)S(1)}, u32[]{:S(2)}, u32[]{:S(2)}) %all-to-all-start.1) | async-done | bytes 2097184 | tf_op jit(solution)/shard_map/all_to_all | solution.py:49
  245.3 4.8 %fusion = f32[16,65536]{1,0:T(8,128)} fusion(f32[1,8,65536]{2,0,1:T(1,128)S(1)} %all-to-all-done.1, s32[8]{0:T(128)S(1)} %get-tuple-element.4), kind=kOutput, calls=%fused_computation.4 | convolution fusion | flops 100663424 | bytes 6291488 | tf_op jit(solution)/shard_map/dot_general | solution.py:52
  250.1 141.2 %all-reduce.3 = bf16[16,65536]{1,0:T(8,128)(2,1)S(1)} all-reduce(f32[16,65536]{1,0:T(8,128)} %fusion), channel_id=1, replica_groups=mesh['pair'=4,'gen'=8] {'pair'}, use_global_device_ids=true, to_apply=%region_1.2 | all-reduce | flops 1048576 | bytes 6291456 | tf_op jit(solution)/shard_map/psum | solution.py:53
  391.4 8.5 %convolution_convert_fusion = bf16[128,65536]{1,0:T(8,128)(2,1)} fusion(bf16[16,128]{1,0:T(8,128)(2,1)S(1)} %convolution_convert_fusion.2, bf16[16,65536]{1,0:T(8,128)(2,1)S(1)} %all-reduce.3), kind=kOutput, calls=%fused_computation.1 | convolution fusion | flops 276824064 | bytes 18878464 | tf_op jit(solution)/shard_map/pe,pc->ec/dot_general | solution.py:54
  399.9 0.0 copy-start.7
  399.9 8.1 %fusion.22 = f32[16,128]{1,0:T(8,128)S(1)} fusion(bf16[16,65536]{1,0:T(8,128)(2,1)S(1)} %all-reduce.3, bf16[128,65536]{1,0:T(8,128)(2,1)} %param.13), kind=kOutput, calls=%fused_computation.40 | convolution fusion | flops 268435456 | bytes 18882560 | tf_op jit(solution)/shard_map/pc,ec->pe/dot_general | solution.py:57
  408.0 12.6 %psum.23 = f32[16,128]{1,0:T(8,128)S(1)} all-reduce(f32[16,128]{1,0:T(8,128)S(1)} %fusion.22), channel_id=1, replica_groups=mesh['pair'=4,'gen'=8] {'gen'}, use_global_device_ids=true, to_apply=%region_2.3 | all-reduce | flops 2048 | bytes 16384 | tf_op jit(solution)/shard_map/psum | solution.py:60
  420.6 0.0 copy-done.7
  420.6 0.0 copy-done.8
  420.6 1.0 fusion.10
  421.6 0.0 copy-done.1
  (3 shorter events, 0.0 us)
Async XLA Ops:
  0.6 1.5 copy-start
  172.7 5.7 %copy-start.4 = (bf16[1024,256]{1,0:T(8,128)(2,1)S(1)}, bf16[1024,256]{1,0:T(8,128)(2,1)}, u32[]{:S(2)}) copy-start(bf16[1024,256]{1,0:T(8,128)(2,1)} %param.8) | copy-start | bytes 1572868
  174.6 19.1 %all-to-all-start = ((bf16[8,2,32768]{2,1,0:T(2,128)(2,1)}), bf16[8,2,32768]{2,1,0:T(2,128)(2,1)S(1)}, u32[]{:S(2)}, u32[]{:S(2)}) async-start(bf16[8,2,32768]{2,1,0:T(2,128)(2,1)} %reshape.166), calls=%async_computation | async-start | bytes 2097152 | tf_op jit(solution)/shard_map/all_to_all | solution.py:32
  201.3 3.9 copy-start.2
  201.3 4.9 %copy-start.5 = (bf16[1024,256]{0,1:T(8,128)(2,1)S(1)}, bf16[1024,256]{0,1:T(8,128)(2,1)}, u32[]{:S(2)}) copy-start(bf16[1024,256]{0,1:T(8,128)(2,1)} %copy.17) | copy-start | bytes 1572868
  201.3 4.9 %copy-start.6 = (bf16[1024,2048]{1,0:T(8,128)(2,1)S(1)}, bf16[1024,2048]{1,0:T(8,128)(2,1)}, u32[]{:S(2)}) copy-start(bf16[1024,2048]{1,0:T(8,128)(2,1)} %param.7) | copy-start | bytes 12582916
  205.2 1.0 copy-start.9
  211.0 8.0 %copy-start.3 = (bf16[2048,256]{1,0:T(8,128)(2,1)S(1)}, bf16[2048,256]{1,0:T(8,128)(2,1)}, u32[]{:S(2)}) copy-start(bf16[2048,256]{1,0:T(8,128)(2,1)} %copy-done.2) | copy-start | bytes 3145732
  215.2 30.2 %all-to-all-start.1 = ((f32[1,8,65536]{2,0,1:T(1,128)}), f32[1,8,65536]{2,0,1:T(1,128)S(1)}, u32[]{:S(2)}, u32[]{:S(2)}) async-start(f32[1,8,65536]{2,0,1:T(1,128)} %all_to_all.20), calls=%async_computation.1 | async-start | bytes 4194304 | tf_op jit(solution)/shard_map/all_to_all | solution.py:49
  399.9 20.7 %copy-start.7 = (s32[16]{0:T(128)S(1)}, s32[16]{0:T(128)}, u32[]{:S(2)}) copy-start(s32[16]{0:T(128)} %param.11) | copy-start | bytes 196
  399.9 20.7 %copy-start.8 = (s32[16]{0:T(128)S(1)}, s32[16]{0:T(128)}, u32[]{:S(2)}) copy-start(s32[16]{0:T(128)} %param.10) | copy-start | bytes 196
  399.9 21.7 %copy-start.1 = (f32[96,128]{1,0:T(8,128)S(1)}, f32[96,128]{1,0:T(8,128)}, u32[]{:S(2)}) copy-start(f32[96,128]{1,0:T(8,128)} %param.12) | copy-start | bytes 147460
where the time goes:
time: 422 us
  blocking collectives  303 us (72%)
  matrix products  45.1 us (11%)
  waiting for transfers between devices  35.7 us (8%)
  local copies, waits for them, and re-layouts  20.8 us (5%)
  other arithmetic  8.67 us (2%)
  starting transfers between devices  7.64 us (2%)
    psum x1, blocking collectives, shards(): adapter_cols = lax.psum(partial_value, 'pair').astype(jnp.bfloat16)  149 us
    psum x1, blocking collectives, shards(): grad_rounded = lax.psum(row_grad, 'pair').astype(jnp.bfloat16)  141 us
    all_to_all x1, waiting for transfers between devices, shards(): lax.all_to_all(outer_grads, 'gen', split_axis=1, concat_axis=0, tiled=True)  21.3 us
    all_to_all x1, waiting for transfers between devices, shards(): lax.all_to_all(outgoing, 'gen', split_axis=1, concat_axis=1, tiled=True)  14.3 us
    psum x1, blocking collectives, shards(): grad_pair = lax.psum(partial_pair, 'gen')  12.6 us
    dot_general x1, matrix products, shards(): jnp.dot(pair_embed, generator, preferred_element_type=jnp.float32)  10.1 us
    dot_general x1, matrix products, shards(): jnp.einsum('pe,pc->ec', pair_embed, grad_rounded, preferred_element_type=...  8.55 us
  transfers between devices with their start and end apart: 2, of which 2 were waited for; matrix products, arithmetic and copies ran while one was open for 1% of the time, Pallas kernels for 0%

commit v1 on v0

--- a/solution.py
+++ b/solution.py
@@ -20,7 +20,7 @@
     ).astype(jnp.float32)
     pair_embed = jnp.dot(hot_both, lang_embed, precision=lax.Precision.HIGHEST).astype(jnp.bfloat16)
     partial_value = jnp.dot(pair_embed, generator, preferred_element_type=jnp.float32)
-    adapter_cols = lax.psum(partial_value, "pair").astype(jnp.bfloat16)
+    adapter_cols = jnp.sum(lax.all_gather(partial_value, "pair"), axis=0).astype(jnp.bfloat16)
     flat_pairs = block_pair[:, 0]
     row_pairs = lax.dynamic_slice_in_dim(
         flat_pairs, pair_index * (gen_count * blocks_here), gen_count * blocks_here

time: 422 us -> 583 us (1.38)
  waiting for transfers between devices: 35.7 us -> 325 us
  blocking collectives: 303 us -> 154 us
  between operations: 0.86 us -> 14.2 us
  other arithmetic: 8.67 us -> 15.1 us
    all_gather x0 -> x1, waiting for transfers between devices: none -> 289 us  [shards(): lax.all_gather(partial_value, 'pair')]
    psum x1 -> x0, blocking collectives: 149 us -> none  [shards(): adapter_cols = lax.psum(partial_value, 'pair').astype(jnp.bfloat16)]
    reduce_sum x0 -> x1, other arithmetic: none -> 7.57 us  [shards(): jnp.sum(lax.all_gather(partial_value, 'pair'), axis=0).astype(jnp.bfloat16)]
  transfers between devices with their start and end apart: 2 -> 3, of which waited for: 2 -> 3; matrix products, arithmetic and copies ran while one was open for 1% -> 1% of each run, Pallas kernels for 0% -> 0%
where the time goes in v1:
time: 583 us
  waiting for transfers between devices  325 us (56%)
  blocking collectives  154 us (26%)
  matrix products  45 us (8%)
  local copies, waits for them, and re-layouts  22.2 us (4%)
  other arithmetic  15.1 us (3%)
  between operations  14.2 us (2%)
  starting transfers between devices  7.52 us (1%)
    all_gather x1, waiting for transfers between devices, shards(): lax.all_gather(partial_value, 'pair')  289 us
    psum x1, blocking collectives, shards(): grad_rounded = lax.psum(row_grad, 'pair').astype(jnp.bfloat16)  141 us
    all_to_all x1, waiting for transfers between devices, shards(): lax.all_to_all(outer_grads, 'gen', split_axis=1, concat_axis=0, tiled=True)  21.4 us
    all_to_all x1, waiting for transfers between devices, shards(): lax.all_to_all(outgoing, 'gen', split_axis=1, concat_axis=1, tiled=True)  14.4 us
    psum x1, blocking collectives, shards(): grad_pair = lax.psum(partial_pair, 'gen')  12.6 us
  transfers between devices with their start and end apart: 3, of which 3 were waited for; matrix products, arithmetic and copies ran while one was open for 1% of the time, Pallas kernels for 0%

profile of v1, /device:TPU:0, one launch (start us, length us, event | category | flops | bytes accessed | tf_op | source)
XLA Modules:
  0.0 582.6 jit_solution(9602623355460629875)
XLA Ops:
  7.2 0.0 copy-start
  7.2 0.0 all-gather.3.cloned.1.call-start
  7.2 0.7 copy-done
  8.0 0.9 convolution_convert_fusion.2
  8.8 10.1 %fusion.21 = f32[16,65536]{1,0:T(8,128)} fusion(bf16[16,128]{1,0:T(8,128)(2,1)S(1)} %convolution_convert_fusion.2, bf16[128,65536]{1,0:T(8,128)(2,1)} %param.13), kind=kOutput, calls=%fused_computation.39 | convolution fusion | flops 268435456 | bytes 20975616 | tf_op jit(solution)/shard_map/dot_general | solution.py:22
  18.9 0.0 all-gather.3.cloned.1.call-update
  19.0 0.6 copy-done.6
  19.6 0.1 fusion.16
  19.7 0.1 compare_and_fusion
  19.8 288.8 %all-gather.3.cloned.1.call-done = f32[64,65536]{1,0:T(8,128)} async-done(((f32[16,65536]{1,0:T(8,128)}), f32[64,65536]{1,0:T(8,128)}) %all-gather.3.cloned.1.call-update) | async-done | bytes 16777232 | tf_op jit(solution)/shard_map/all_gather | solution.py:23
  308.6 7.6 %reduce_sum.9 = bf16[16,65536]{1,0:T(8,128)(2,1)S(1)} reduce(f32[4,16,65536]{2,1,0:T(8,128)} %bitcast.34, f32[]{:T(128)} %constant.29.clone.1), dimensions={0}, to_apply=%region_0.0 | reduce | flops 3145728 | bytes 18874372 | tf_op jit(solution)/shard_map/reduce_sum | solution.py:23
  316.2 1.2 gather_fusion
  317.4 0.2 bitcast_select_fusion
  317.6 1.6 copy.27
  319.2 0.5 broadcast.100
  319.7 7.2 %reduce.2 = bf16[8,65536]{1,0:T(8,128)(2,1)S(1)} reduce(bf16[8,1,65536]{2,1,0:T(2,128)(2,1)S(1)} %bitcast.35, bf16[]{:T(256)} %broadcast.100), dimensions={1}, to_apply=%bitcast.33.reduce_sub_computation | reduce | bytes 2097154
  327.0 0.0 copy-start.4
  327.0 1.9 reshape.167
  328.8 3.7 all-to-all-start
  332.5 0.0 copy-done.4
  332.5 1.0 copy.17
  333.5 14.4 %all-to-all-done = bf16[8,2,32768]{2,1,0:T(2,128)(2,1)S(1)} async-done(((bf16[8,2,32768]{2,1,0:T(2,128)(2,1)}), bf16[8,2,32768]{2,1,0:T(2,128)(2,1)S(1)}, u32[]{:S(2)}, u32[]{:S(2)}) %all-to-all-start) | async-done | bytes 1048608 | tf_op jit(solution)/shard_map/all_to_all | solution.py:32
  347.9 1.0 reshape.168
  348.9 6.0 %bitcast_reduce_fusion = bf16[8,65536]{1,0:T(8,128)(2,1)S(1)} fusion(bf16[8,1,65536]{2,1,0:T(2,128)(2,1)S(1)} %reshape.168), kind=kLoop, calls=%fused_computation.37 | loop fusion | bytes 2097152 | tf_op jit(solution)/shard_map/all_to_all | solution.py:32
  354.9 0.5 reshape.156
  355.4 0.0 copy-start.2
  355.4 0.0 copy-start.5
  355.4 0.0 copy-start.7
  355.5 3.9 convolution_bitcast_fusion.1
  359.4 0.0 copy-done.2
  359.4 0.0 copy-start.10
  359.4 1.0 copy-done.10
  360.3 0.0 copy-done.5
  360.3 0.0 copy-done.7
  360.3 2.9 convolution_bitcast_fusion
  363.2 1.9 copy.19
  365.1 0.0 copy-start.3
  365.1 4.2 all_to_all.20
  369.3 3.8 all-to-all-start.1
  373.1 0.0 copy-done.3
  373.1 5.0 convolution_convert_fusion.1
  378.1 21.4 %all-to-all-done.1 = f32[1,8,65536]{2,0,1:T(1,128)S(1)} async-done(((f32[1,8,65536]{2,0,1:T(1,128)}), f32[1,8,65536]{2,0,1:T(1,128)S(1)}, u32[]{:S(2)}, u32[]{:S(2)}) %all-to-all-start.1) | async-done | bytes 2097184 | tf_op jit(solution)/shard_map/all_to_all | solution.py:49
  399.5 4.8 fusion
  404.3 141.2 %all-reduce.1 = bf16[16,65536]{1,0:T(8,128)(2,1)S(1)} all-reduce(f32[16,65536]{1,0:T(8,128)} %fusion), channel_id=1, replica_groups=mesh['pair'=4,'gen'=8] {'pair'}, use_global_device_ids=true, to_apply=%region_1.2 | all-reduce | flops 1048576 | bytes 6291456 | tf_op jit(solution)/shard_map/psum | solution.py:53
  545.5 8.5 %convolution_convert_fusion = bf16[128,65536]{1,0:T(8,128)(2,1)} fusion(bf16[16,128]{1,0:T(8,128)(2,1)S(1)} %convolution_convert_fusion.2, bf16[16,65536]{1,0:T(8,128)(2,1)S(1)} %all-reduce.1), kind=kOutput, calls=%fused_computation.1 | convolution fusion | flops 276824064 | bytes 18878464 | tf_op jit(solution)/shard_map/pe,pc->ec/dot_general | solution.py:54
  554.1 8.1 %fusion.22 = f32[16,128]{1,0:T(8,128)S(1)} fusion(bf16[16,65536]{1,0:T(8,128)(2,1)S(1)} %all-reduce.1, bf16[128,65536]{1,0:T(8,128)(2,1)} %param.13), kind=kOutput, calls=%fused_computation.40 | convolution fusion | flops 268435456 | bytes 18882560 | tf_op jit(solution)/shard_map/pc,ec->pe/dot_general | solution.py:57
  562.1 12.6 %psum.15 = f32[16,128]{1,0:T(8,128)S(1)} all-reduce(f32[16,128]{1,0:T(8,128)S(1)} %fusion.22), channel_id=1, replica_groups=mesh['pair'=4,'gen'=8] {'gen'}, use_global_device_ids=true, to_apply=%region_2.3 | all-reduce | flops 2048 | bytes 16384 | tf_op jit(solution)/shard_map/psum | solution.py:60
  574.8 1.0 fusion.10
  (8 shorter events, 0.0 us)
Async XLA Ops:
  7.2 0.8 copy-start
  7.2 301.4 %all-gather.3.cloned.1.call-start = ((), (), s32[]{:S(2)}) async-start(), calls=%async_computation.2 | async-start | bytes 20971520 | tf_op jit(solution)/shard_map/all_gather | solution.py:23
  18.9 0.7 copy-start.6
  327.0 5.5 copy-start.4
  328.8 19.1 %all-to-all-start = ((bf16[8,2,32768]{2,1,0:T(2,128)(2,1)}), bf16[8,2,32768]{2,1,0:T(2,128)(2,1)S(1)}, u32[]{:S(2)}, u32[]{:S(2)}) async-start(bf16[8,2,32768]{2,1,0:T(2,128)(2,1)} %reshape.167), calls=%async_computation | async-start | bytes 2097152 | tf_op jit(solution)/shard_map/all_to_all | solution.py:32
  355.4 3.9 copy-start.2
  355.4 4.9 copy-start.5
  355.4 4.9 copy-start.7
  359.4 1.0 copy-start.10
  365.1 8.0 %copy-start.3 = (bf16[2048,256]{1,0:T(8,128)(2,1)S(1)}, bf16[2048,256]{1,0:T(8,128)(2,1)}, u32[]{:S(2)}) copy-start(bf16[2048,256]{1,0:T(8,128)(2,1)} %copy-done.2) | copy-start | bytes 3145732
  369.3 30.2 %all-to-all-start.1 = ((f32[1,8,65536]{2,0,1:T(1,128)}), f32[1,8,65536]{2,0,1:T(1,128)S(1)}, u32[]{:S(2)}, u32[]{:S(2)}) async-start(f32[1,8,65536]{2,0,1:T(1,128)} %all_to_all.20), calls=%async_computation.1 | async-start | bytes 4194304 | tf_op jit(solution)/shard_map/all_to_all | solution.py:49
  554.1 20.7 %copy-start.8 = (s32[16]{0:T(128)S(1)}, s32[16]{0:T(128)}, u32[]{:S(2)}) copy-start(s32[16]{0:T(128)} %param.11) | copy-start | bytes 196
  554.1 20.7 %copy-start.9 = (s32[16]{0:T(128)S(1)}, s32[16]{0:T(128)}, u32[]{:S(2)}) copy-start(s32[16]{0:T(128)} %param.10) | copy-start | bytes 196
  554.1 21.7 %copy-start.1 = (f32[96,128]{1,0:T(8,128)S(1)}, f32[96,128]{1,0:T(8,128)}, u32[]{:S(2)}) copy-start(f32[96,128]{1,0:T(8,128)} %param.12) | copy-start | bytes 147460
Sparse Core Ops, SparseCore 0:
  19.1 289.4 all-gather.2
